TPU v7x, 128 devices: a whole 4x4x4 slice. The times are simulated.
128 devices in a mesh: fsdp: 8 (over x, z_lo), dp: 16 (over z_hi, y, core).
Axes of the slice: x: 4, y: 4, z: 4 (z_hi: 2, z_lo: 2; z = z_hi * 2 + z_lo), core: 2. Of those that a mesh axis runs over, the one named last changes fastest.
Arguments:
- tokens: bfloat16 [8, 2176, 3200], P('fsdp', 'dp'), may hold values from -6 to 6
- norm_gain: float32 [3200], replicated, may hold values from 0.5 to 1.5
- qkv_weight: bfloat16 [3200, 6144], P('fsdp', 'dp'), may hold values from -4 to 4
- qk_gain: float32 [2, 2048], P(None, 'dp'), may hold values from 1 to 8
- out_weight: bfloat16 [2048, 3200], P('dp', 'fsdp'), may hold values from -0.125 to 0.125
- layer_scale: float32 [3200], replicated, may hold values from 0.2 to 1
- tile_counts: int32 [8, 2], replicated, may hold values from 0 to 2, as said below
- owners: int32 [8, 2], replicated, may hold values from 0 to 7, as said below
Outputs:
- vision_tokens: bfloat16 [32, 256, 12800], P('fsdp', None, 'dp')
Inputs may be any that keep to these rules, and one draw needn't show every extreme that they name: `tile_counts`: column 0 is 1 to 2, column 1 is 0 to 2 minus column 0. All owners together get at most 4 live tiles each, and one owner gets exactly 4.
All inputs are finite; a program needn't handle non-finite values.
Results may differ from a plain program's by a relative error of at most 0.006.
The roundings to bfloat16 on the way count: a program that leaves them out, or rounds other values in their place, can miss the bound.
Values may be sent and summed in bfloat16 or wider, within the bound.
No kernel may reach another device: no remote copies, remote signals or barrier semaphores. Data moves between devices by JAX's collectives and lax.ppermute only.
A program may use at most 192 MiB of HBM per device.

v0:
```python
import jax
import jax.numpy as jnp
from jax import lax
from jax.sharding import PartitionSpec as P

HEAD_DIM = 128
GRID = 32
SLOTS = 2
TILE = 1025
CAP = 4
EPSILON = 1e-06


def merge_tiles(values):
    halves = GRID // 2
    columns = values.shape[1]
    tile_list = []
    for tile_slot in range(SLOTS):
        patches = values[tile_slot * TILE + 1 : (tile_slot + 1) * TILE]
        square = patches.reshape(halves, 2, halves, 2, columns).transpose(0, 2, 4, 1, 3)
        tile_list.append(square.reshape(halves * halves, columns * 4))
    return jnp.stack(tile_list)


def tile_owners(tile_counts, owners):
    slot_index = jnp.arange(SLOTS, dtype=jnp.int32)[None, :]
    first_count = tile_counts[:, 0:1]
    holder = jnp.where(slot_index < first_count, owners[:, 0:1], owners[:, 1:2])
    living = slot_index < first_count + tile_counts[:, 1:2]
    return (holder, living)


def place_tiles(received, holder, living, target):
    owned_flag = jnp.logical_and(living, holder == target).reshape(-1).astype(jnp.int32)
    before = jnp.cumsum(owned_flag) - owned_flag
    chosen = jnp.logical_and(
        before[None, :] == jnp.arange(CAP, dtype=jnp.int32)[:, None], owned_flag[None, :] == 1
    )
    flattened = received.reshape(received.shape[0] * received.shape[1], -1)
    placed = jnp.dot(chosen.astype(jnp.bfloat16), flattened, preferred_element_type=jnp.float32)
    return placed.astype(jnp.bfloat16).reshape(CAP, received.shape[2], received.shape[3])


def body(tokens, norm_gain, qkv_weight, qk_gain, out_weight, layer_scale, tile_counts, owners):
    own_rows = tokens[0]
    gathered = lax.all_gather(own_rows, "dp", axis=0, tiled=True)
    length = gathered.shape[0]
    model_width = gathered.shape[1]
    groups = lax.axis_size("dp")
    values = gathered.astype(jnp.float32)
    normed = (
        values * lax.rsqrt(jnp.mean(values * values, axis=-1, keepdims=True) + EPSILON) * norm_gain
    ).astype(jnp.bfloat16)
    projected = jnp.dot(
        normed,
        lax.all_gather(qkv_weight, "fsdp", axis=0, tiled=True),
        preferred_element_type=jnp.float32,
    )
    queries = projected[:, :HEAD_DIM]
    keys_part = projected[:, HEAD_DIM : 2 * HEAD_DIM]
    values_part = projected[:, 2 * HEAD_DIM :].astype(jnp.bfloat16)
    query_sums, key_sums = lax.psum(
        (jnp.sum(queries * queries, axis=-1), jnp.sum(keys_part * keys_part, axis=-1)), "dp"
    )
    window = groups * HEAD_DIM
    queries = (queries * lax.rsqrt(query_sums / window + EPSILON)[:, None] * qk_gain[0]).astype(
        jnp.bfloat16
    )
    keys_part = (keys_part * lax.rsqrt(key_sums / window + EPSILON)[:, None] * qk_gain[1]).astype(
        jnp.bfloat16
    )
    row_index = lax.axis_index("fsdp")
    row_count = lax.axis_size("fsdp")
    factor = HEAD_DIM ** (-0.5)
    covered = SLOTS * TILE
    tile_query = queries[:covered].reshape(SLOTS, TILE, HEAD_DIM)
    tile_key = keys_part[:covered].reshape(SLOTS, TILE, HEAD_DIM)
    tile_value = values_part[:covered].reshape(SLOTS, TILE, HEAD_DIM)
    scores = (
        jnp.einsum("sqc,skc->sqk", tile_query, tile_key, preferred_element_type=jnp.float32)
        * factor
    )
    highest = jnp.max(scores, axis=-1, keepdims=True)
    exponent = jnp.exp(scores - highest)
    weights = (exponent / jnp.sum(exponent, axis=-1, keepdims=True)).astype(jnp.bfloat16)
    tile_out = jnp.einsum(
        "sqk,skc->sqc", weights, tile_value, preferred_element_type=jnp.float32
    ).astype(jnp.bfloat16)
    head_out = jnp.concatenate(
        [
            tile_out.reshape(covered, HEAD_DIM),
            jnp.zeros((length - covered, HEAD_DIM), jnp.bfloat16),
        ],
        axis=0,
    )
    dp_index = lax.axis_index("dp")
    block = model_width // groups
    head_rows = lax.all_gather(out_weight, "fsdp", axis=1, tiled=True)
    weight_block = lax.all_to_all(head_rows, "dp", split_axis=1, concat_axis=0, tiled=True)
    all_heads = lax.all_gather(head_out, "dp", axis=0, tiled=False)
    head_terms = jnp.einsum(
        "hsc,hcd->hsd",
        all_heads,
        weight_block.reshape(groups, HEAD_DIM, block),
        preferred_element_type=jnp.float32,
    ).astype(jnp.bfloat16)
    attention = jnp.sum(lax.optimization_barrier(head_terms).astype(jnp.float32), axis=0)
    own_block = lax.dynamic_slice_in_dim(gathered, dp_index * block, block, axis=1)
    scale_block = lax.dynamic_slice_in_dim(layer_scale, dp_index * block, block)
    updated = (own_block.astype(jnp.float32) + scale_block * attention).astype(jnp.bfloat16)
    merged = merge_tiles(updated)
    holder, living = tile_owners(tile_counts, owners)
    own_holder = holder[row_index]
    own_living = living[row_index]
    destination = jnp.arange(row_count, dtype=jnp.int32)[:, None]
    sending = jnp.logical_and(destination == own_holder[None, :], own_living[None, :])
    outgoing = jnp.where(sending[:, :, None, None], merged[None], jnp.zeros((), jnp.bfloat16))
    received = lax.all_to_all(outgoing, "fsdp", split_axis=0, concat_axis=0, tiled=True)
    return place_tiles(received, holder, living, row_index)


def solution(mesh):
    placed = (
        P("fsdp", "dp", None),
        P(),
        P("fsdp", "dp"),
        P(None, "dp"),
        P("dp", "fsdp"),
        P(),
        P(),
        P(),
    )
    return jax.shard_map(
        body, mesh=mesh, in_specs=placed, out_specs=P("fsdp", None, "dp"), check_vma=False
    )
```

profile of v0, /device:TPU:1, one launch (start us, length us, event | category | flops | bytes accessed | tf_op | source)
XLA Modules:
  0.0 529.9 jit_solution(8321030742287554255)
XLA Ops:
  6.5 0.0 all-gather.8.cloned.1.call-start
  6.5 0.7 all-gather.8.cloned.1.call-update
  7.3 0.0 all-gather.6.cloned.1.call-start
  7.3 0.7 all-gather.6.cloned.1.call-update
  8.0 0.0 all-gather.10.cloned.1.call-start
  8.1 0.8 slice_bitcast_fusion
  8.8 101.3 %all-gather.8.cloned.1.call-done = bf16[1,2176,3200]{2,1,0:T(8,128)(2,1)} async-done(((bf16[1,136,3200]{2,1,0:T(8,128)(2,1)}), bf16[1,2176,3200]{2,1,0:T(8,128)(2,1)}) %all-gather.8.cloned.1.call-update) | async-done | bytes 13926416 | tf_op jit(solution)/shard_map/all_gather | solution.py:46
  110.2 7.7 %fusion.1 = f32[2176]{0:T(1024)S(1)} fusion(bf16[1,2176,3200]{2,1,0:T(8,128)(2,1)} %all-gather.8.cloned.1.call-done), kind=kLoop, calls=%fused_computation.4 | loop fusion | flops 20887424 | bytes 13935104 | tf_op jit(solution)/shard_map/reduce_sum | solution.py:52
  117.9 47.7 %all-gather.6.cloned.1.call-done = bf16[3200,384]{1,0:T(8,128)(2,1)} async-done(((bf16[400,384]{1,0:T(8,128)(2,1)}), bf16[3200,384]{1,0:T(8,128)(2,1)}) %all-gather.6.cloned.1.call-update) | async-done | bytes 2457616 | tf_op jit(solution)/shard_map/all_gather | solution.py:56
  165.6 0.0 copy-done.4
  165.6 11.8 %fusion.5 = f32[2176,384]{1,0:T(8,128)S(1)} fusion(bf16[3200,384]{1,0:T(8,128)(2,1)} %all-gather.6.cloned.1.call-done, bf16[1,2176,3200]{2,1,0:T(8,128)(2,1)} %all-gather.8.cloned.1.call-done, f32[3200]{0:T(1024)S(1)} %copy-done.4, f32[2176]{0:T(1024)S(1)} %add_rsqrt_fusion.2), kind=kOutput, calls=%fused_computation.11 | convolution fusion | flops 5375590400 | bytes 19747840 | tf_op jit(solution)/shard_map/dot_general | solution.py:54
  177.5 0.1 slice.84
  177.5 0.6 multiply_reduce_fusion
  178.2 65.0 %all-reduce.1 = (f32[2176]{0:T(1024)S(1)}, f32[2176]{0:T(1024)S(1)}) all-reduce(f32[2176]{0:T(1024)S(1)} %get-tuple-element.6, f32[2176]{0:T(1024)S(1)} %get-tuple-element.5), channel_id=1, replica_groups=mesh['fsdp'=8,'dp'=16] {'dp'}, use_global_device_ids=true, to_apply=%region_3.0 | all-reduce | flops 4352 | bytes 34816 | tf_op jit(solution)/shard_map/psum | solution.py:62
  243.2 0.9 reshape.243
  244.1 1.1 fusion.15
  245.2 0.1 reshape.242
  245.3 0.0 copy-start
  245.3 0.1 reshape.241
  245.5 3.2 fusion.32
  248.7 0.0 copy-done
  248.7 0.0 copy-start.1
  248.7 0.0 copy-start.2
  248.7 0.0 copy-start.3
  248.7 4.9 fusion.12
  253.6 0.1 reshape.244
  253.7 0.8 concatenate.3
  254.6 0.0 all-gather.10.cloned.1.call-update
  254.6 0.0 copy-done.1
  254.6 27.5 %all_gather.19 = bf16[128,3200]{0,1:T(8,128)(2,1)} all-gather(bf16[128,400]{0,1:T(8,128)(2,1)S(1)} %copy-done.1), channel_id=1, replica_groups=mesh['fsdp'=8,'dp'=16] {'fsdp'}, dimensions={1}, use_global_device_ids=true | all-gather | bytes 921600 | tf_op jit(solution)/shard_map/all_gather | solution.py:98
  282.1 15.1 %all-to-all-start = ((bf16[128,16,200]{0,2,1:T(8,128)(2,1)}), bf16[128,16,200]{0,2,1:T(8,128)(2,1)S(1)}, u32[]{:S(2)}, u32[]{:S(2)}) async-start(bf16[128,16,200]{0,2,1:T(8,128)(2,1)} %bitcast.12), calls=%async_computation | async-start | bytes 1638400 | tf_op jit(solution)/shard_map/all_to_all | solution.py:99
  297.2 0.0 copy-done.2
  297.2 0.1 fusion.19
  297.3 0.1 and_convert_fusion
  297.4 0.8 dynamic_slice.15
  298.2 2.5 constant_dynamic-slice_fusion
  300.7 0.8 copy.37
  301.5 14.2 %all-to-all-done = bf16[128,16,200]{0,2,1:T(8,128)(2,1)S(1)} async-done(((bf16[128,16,200]{0,2,1:T(8,128)(2,1)}), bf16[128,16,200]{0,2,1:T(8,128)(2,1)S(1)}, u32[]{:S(2)}, u32[]{:S(2)}) %all-to-all-start) | async-done | bytes 819232 | tf_op jit(solution)/shard_map/all_to_all | solution.py:99
  315.7 31.7 %all-gather.10.cloned.1.call-done = bf16[34816,128]{1,0:T(8,128)(2,1)} async-done(((bf16[2176,128]{1,0:T(8,128)(2,1)}), bf16[34816,128]{1,0:T(8,128)(2,1)}) %all-gather.10.cloned.1.call-update) | async-done | bytes 8912912 | tf_op jit(solution)/shard_map/all_gather | solution.py:100
  347.3 10.8 %convolution_convert_fusion.1 = bf16[16,2176,200]{1,2,0:T(8,128)(2,1)} fusion(bf16[16,2176,128]{2,1,0:T(8,128)(2,1)} %bitcast.53, bf16[128,16,200]{0,2,1:T(8,128)(2,1)S(1)} %all-to-all-done), kind=kOutput, calls=%fused_computation.8 | convolution fusion | flops 1789542400 | bytes 23658496 | tf_op jit(solution)/shard_map/hsc,hcd->hsd/dot_general | solution.py:101
  358.2 7.3 %convert_reduce_fusion = f32[2176,200]{0,1:T(8,128)S(1)} fusion(bf16[16,2176,200]{1,2,0:T(8,128)(2,1)} %convolution_convert_fusion.1), kind=kLoop, calls=%fused_computation.7 | loop fusion | flops 13491200 | bytes 15667200 | tf_op jit(solution)/shard_map/reduce_sum | solution.py:107
  365.5 0.3 fusion.13
  365.8 0.4 fusion.31
  366.1 0.2 copy.30
  366.4 1.0 reshape.245
  367.4 0.2 copy.32
  367.6 1.1 reshape.246
  368.7 4.9 copy.33
  373.5 3.9 stack_reshape.7
  377.4 4.9 copy.31
  382.3 3.8 stack_reshape.6
  386.1 1.2 pad_maximum_fusion
  387.3 3.3 broadcast_select_fusion
  390.7 5.0 all-to-all-start.1
  395.6 0.1 reshape.250
  395.7 0.1 reshape.256
  395.8 0.1 reduce
  396.0 90.6 %all-to-all-done.1 = bf16[8,2,256,800]{2,3,1,0:T(8,128)(2,1)} async-done(((bf16[8,2,256,800]{2,3,1,0:T(8,128)(2,1)}), bf16[8,2,256,800]{2,3,1,0:T(8,128)(2,1)}, u32[]{:S(2)}, u32[]{:S(2)}) %all-to-all-start.1) | async-done | bytes 6553632 | tf_op jit(solution)/shard_map/all_to_all | solution.py:118
  486.6 11.1 %copy.34 = bf16[8,2,256,800]{3,2,1,0:T(8,128)(2,1)} copy(bf16[8,2,256,800]{2,3,1,0:T(8,128)(2,1)} %all-to-all-done.1) | data formatting | bytes 13107200 | tf_op jit(solution)/shard_map/all_to_all | solution.py:118
  497.7 14.7 %reshape.247 = bf16[16,204800]{1,0:T(8,128)(2,1)} reshape(bf16[8,2,256,800]{3,2,1,0:T(8,128)(2,1)} %copy.34) | data formatting | bytes 13107200 | tf_op jit(solution)/shard_map/reshape | solution.py:39
  512.4 4.0 convolution_convert_fusion
  516.4 1.6 reshape.258
  518.0 2.8 reshape.248
  520.8 2.3 copy.35
  (12 shorter events, 0.1 us)
Async XLA Ops:
  6.5 103.6 %all-gather.8.cloned.1.call-start = ((), (), s32[]{:S(2)}) async-start(), calls=%async_computation.3 | async-start | bytes 14796800 | tf_op jit(solution)/shard_map/all_gather | solution.py:46
  7.3 158.4 %all-gather.6.cloned.1.call-start = ((), (), s32[]{:S(2)}) async-start(), calls=%async_computation.2 | async-start | bytes 2764800 | tf_op jit(solution)/shard_map/all_gather | solution.py:56
  8.0 339.3 %all-gather.10.cloned.1.call-start = ((), (), s32[]{:S(2)}) async-start(), calls=%async_computation.4 | async-start | bytes 9469952 | tf_op jit(solution)/shard_map/all_gather | solution.py:100
  8.8 156.8 %copy-start.4 = (f32[3200]{0:T(1024)S(1)}, f32[3200]{0:T(1024)}, u32[]{:S(2)}) copy-start(f32[3200]{0:T(1024)} %param.9) | copy-start | bytes 38404
  245.3 3.4 copy-start
  248.7 5.9 %copy-start.1 = (bf16[128,400]{0,1:T(8,128)(2,1)S(1)}, bf16[128,400]{0,1:T(8,128)(2,1)}, u32[]{:S(2)}) copy-start(bf16[128,400]{0,1:T(8,128)(2,1)} %param.12) | copy-start | bytes 307204
  248.7 48.5 %copy-start.2 = (s32[8,2]{0,1:T(2,128)S(1)}, s32[8,2]{0,1:T(2,128)}, u32[]{:S(2)}) copy-start(s32[8,2]{0,1:T(2,128)} %param.15) | copy-start | bytes 196
  248.7 48.5 %copy-start.3 = (s32[8,2]{0,1:T(2,128)S(1)}, s32[8,2]{0,1:T(2,128)}, u32[]{:S(2)}) copy-start(s32[8,2]{0,1:T(2,128)} %param.14) | copy-start | bytes 196
  282.1 33.6 %all-to-all-start = ((bf16[128,16,200]{0,2,1:T(8,128)(2,1)}), bf16[128,16,200]{0,2,1:T(8,128)(2,1)S(1)}, u32[]{:S(2)}, u32[]{:S(2)}) async-start(bf16[128,16,200]{0,2,1:T(8,128)(2,1)} %bitcast.12), calls=%async_computation | async-start | bytes 1638400 | tf_op jit(solution)/shard_map/all_to_all | solution.py:99
  390.7 95.9 %all-to-all-start.1 = ((bf16[8,2,256,800]{2,3,1,0:T(8,128)(2,1)}), bf16[8,2,256,800]{2,3,1,0:T(8,128)(2,1)}, u32[]{:S(2)}, u32[]{:S(2)}) async-start(bf16[8,2,256,800]{2,3,1,0:T(8,128)(2,1)} %broadcast_select_fusion), calls=%async_computation.1 | async-start | bytes 13107200 | tf_op jit(solution)/shard_map/all_to_all | solution.py:118
Sparse Core Ops, SparseCore 0:
  9.8 100.3 all-gather.7
  111.8 53.8 all-gather.5
  254.7 92.5 all-gather.9
where the time goes:
time: 535 us; the launch traced here: 530 us
  waiting for transfers between devices  287 us (54%)
  blocking collectives  92.5 us (17%)
  local copies, waits for them, and re-layouts  59.9 us (11%)
  matrix products  34.7 us (6%)
  other arithmetic  22 us (4%)
  starting transfers between devices  20.1 us (4%)
  between operations  13.6 us (3%)
    all_gather x1, waiting for transfers between devices, body(): gathered = lax.all_gather(own_rows, 'dp', axis=0, tiled=True)  101 us
    all_to_all x1, waiting for transfers between devices, body(): lax.all_to_all(outgoing, 'fsdp', split_axis=0, concat_axis=0, tiled=True)  90.6 us
    psum x1, blocking collectives, body(): lax.psum((jnp.sum(queries * queries, axis=-1), jnp.sum(keys_part * keys_p...  65 us
    all_gather x1, waiting for transfers between devices, body(): lax.all_gather(qkv_weight, 'fsdp', axis=0, tiled=True)  47.7 us
    all_gather x1, waiting for transfers between devices, body(): all_heads = lax.all_gather(head_out, 'dp', axis=0, tiled=False)  31.7 us
    all_gather x1, blocking collectives, body(): head_rows = lax.all_gather(out_weight, 'fsdp', axis=1, tiled=True)  27.5 us
    all_to_all x1, starting transfers between devices, body(): lax.all_to_all(head_rows, 'dp', split_axis=1, concat_axis=0, tiled=True)  15.1 us
    reshape x1, local copies, waits for them, and re-layouts, place_tiles(): flattened = received.reshape(received.shape[0] * received.shape[1], -1)  14.7 us
  transfers between devices with their start and end apart: 5, of which 5 were waited for; matrix products, arithmetic and copies ran while one was open for 2% of the time, Pallas kernels for 0%

commit v1 on v0

--- a/solution.py
+++ b/solution.py
@@ -96,7 +96,11 @@
     dp_index = lax.axis_index("dp")
     block = model_width // groups
     head_rows = lax.all_gather(out_weight, "fsdp", axis=1, tiled=True)
-    weight_block = lax.all_to_all(head_rows, "dp", split_axis=1, concat_axis=0, tiled=True)
+    base_arr = lax.axis_size("dp")
+    part_next = jnp.split(head_rows, base_arr, axis=1)
+    seen_now = jnp.stack(part_next, axis=0)
+    r2 = lax.all_to_all(seen_now, "dp", 0, 0)
+    weight_block = jnp.concatenate(r2, axis=0)
     all_heads = lax.all_gather(head_out, "dp", axis=0, tiled=False)
     head_terms = jnp.einsum(
         "hsc,hcd->hsd",

time: 535 us -> 535 us (level)
  local copies, waits for them, and re-layouts: 59.9 us -> 69.4 us
  waiting for transfers between devices: 287 us -> 279 us
    unnamed x12 -> x27, local copies, waits for them, and re-layouts: 2.47 us -> 11.8 us
    all_gather x1, waiting for transfers between devices: 31.7 us -> 25.5 us  [body(): all_heads = lax.all_gather(head_out, 'dp', axis=0, tiled=False)]
  transfers between devices with their start and end apart: 5 -> 5, of which waited for: 5 -> 5; matrix products, arithmetic and copies ran while one was open for 2% -> 4% of each run, Pallas kernels for 0% -> 0%
where the time goes in v1:
time: 535 us; the launch traced here: 529 us
  waiting for transfers between devices  279 us (52%)
  blocking collectives  90.4 us (17%)
  local copies, waits for them, and re-layouts  69.4 us (13%)
  matrix products  34.7 us (6%)
  other arithmetic  22 us (4%)
  starting transfers between devices  20.6 us (4%)
  between operations  13.6 us (3%)
    all_gather x1, waiting for transfers between devices, body(): gathered = lax.all_gather(own_rows, 'dp', axis=0, tiled=True)  101 us
    all_to_all x1, waiting for transfers between devices, body(): lax.all_to_all(outgoing, 'fsdp', split_axis=0, concat_axis=0, tiled=True)  90.6 us
    psum x1, blocking collectives, body(): lax.psum((jnp.sum(queries * queries, axis=-1), jnp.sum(keys_part * keys_p...  65 us
    all_gather x1, waiting for transfers between devices, body(): lax.all_gather(qkv_weight, 'fsdp', axis=0, tiled=True)  47.7 us
    all_gather x1, waiting for transfers between devices, body(): all_heads = lax.all_gather(head_out, 'dp', axis=0, tiled=False)  25.5 us
    all_gather x1, blocking collectives, body(): head_rows = lax.all_gather(out_weight, 'fsdp', axis=1, tiled=True)  25.4 us
    all_to_all x1, starting transfers between devices, body(): r2 = lax.all_to_all(seen_now, 'dp', 0, 0)  15.6 us
    reshape x1, local copies, waits for them, and re-layouts, place_tiles(): flattened = received.reshape(received.shape[0] * received.shape[1], -1)  14.7 us
  transfers between devices with their start and end apart: 5, of which 5 were waited for; matrix products, arithmetic and copies ran while one was open for 4% of the time, Pallas kernels for 0%

profile of v1, /device:TPU:1, one launch (start us, length us, event | category | flops | bytes accessed | tf_op | source)
XLA Modules:
  0.0 529.3 jit_solution(11174070470616331768)
XLA Ops:
  6.5 0.7 all-gather.8.cloned.1.call-update
  7.3 0.7 all-gather.6.cloned.1.call-update
  8.1 0.8 slice_bitcast_fusion.16
  8.8 101.3 %all-gather.8.cloned.1.call-done = bf16[1,2176,3200]{2,1,0:T(8,128)(2,1)} async-done(((bf16[1,136,3200]{2,1,0:T(8,128)(2,1)}), bf16[1,2176,3200]{2,1,0:T(8,128)(2,1)}) %all-gather.8.cloned.1.call-update) | async-done | bytes 13926416 | tf_op jit(solution)/shard_map/all_gather | solution.py:46
  110.2 7.7 %fusion.1 = f32[2176]{0:T(1024)S(1)} fusion(bf16[1,2176,3200]{2,1,0:T(8,128)(2,1)} %all-gather.8.cloned.1.call-done), kind=kLoop, calls=%fused_computation.4 | loop fusion | flops 20887424 | bytes 13935104 | tf_op jit(solution)/shard_map/reduce_sum | solution.py:52
  117.9 47.7 %all-gather.6.cloned.1.call-done = bf16[3200,384]{1,0:T(8,128)(2,1)} async-done(((bf16[400,384]{1,0:T(8,128)(2,1)}), bf16[3200,384]{1,0:T(8,128)(2,1)}) %all-gather.6.cloned.1.call-update) | async-done | bytes 2457616 | tf_op jit(solution)/shard_map/all_gather | solution.py:56
  165.6 11.8 %fusion.5 = f32[2176,384]{1,0:T(8,128)S(1)} fusion(bf16[3200,384]{1,0:T(8,128)(2,1)} %all-gather.6.cloned.1.call-done, bf16[1,2176,3200]{2,1,0:T(8,128)(2,1)} %all-gather.8.cloned.1.call-done, f32[3200]{0:T(1024)S(1)} %copy-done.4, f32[2176]{0:T(1024)S(1)} %add_rsqrt_fusion.2), kind=kOutput, calls=%fused_computation.11 | convolution fusion | flops 5375590400 | bytes 19747840 | tf_op jit(solution)/shard_map/dot_general | solution.py:54
  177.5 0.6 multiply_reduce_fusion
  178.2 65.0 %all-reduce.1 = (f32[2176]{0:T(1024)S(1)}, f32[2176]{0:T(1024)S(1)}) all-reduce(f32[2176]{0:T(1024)S(1)} %get-tuple-element.6, f32[2176]{0:T(1024)S(1)} %get-tuple-element.5), channel_id=1, replica_groups=mesh['fsdp'=8,'dp'=16] {'dp'}, use_global_device_ids=true, to_apply=%region_3.0 | all-reduce | flops 4352 | bytes 34816 | tf_op jit(solution)/shard_map/psum | solution.py:62
  243.2 0.9 reshape.238
  244.1 1.1 fusion.15
  245.2 0.1 reshape.237
  245.3 0.1 reshape.236
  245.5 3.2 fusion.47
  248.7 4.9 fusion.12
  253.6 0.1 reshape.239
  253.7 0.9 concatenate.3
  254.6 25.4 %all_gather.19 = bf16[128,3200]{0,1:T(8,128)(2,1)S(1)} all-gather(bf16[128,400]{0,1:T(8,128)(2,1)S(1)} %copy-done.1), channel_id=1, replica_groups=mesh['fsdp'=8,'dp'=16] {'fsdp'}, dimensions={1}, use_global_device_ids=true | all-gather | bytes 921600 | tf_op jit(solution)/shard_map/all_gather | solution.py:98
  280.0 0.6 fusion.33
  280.6 0.6 fusion.32
  281.3 0.6 fusion.31
  281.9 0.6 fusion.30
  282.5 0.6 fusion.29
  283.1 0.6 fusion.28
  283.8 0.6 fusion.27
  284.4 0.6 fusion.26
  285.0 0.6 fusion.25
  285.6 0.6 fusion.24
  286.3 0.6 fusion.23
  286.9 0.6 fusion.22
  287.5 0.6 fusion.21
  288.1 0.6 fusion.20
  288.8 0.6 fusion.19
  289.4 0.6 fusion.18
  290.0 15.6 %all-to-all-start = ((bf16[16,128,200]{1,2,0:T(8,128)(2,1)}), bf16[16,128,200]{1,2,0:T(8,128)(2,1)S(1)}, u32[]{:S(2)}, u32[]{:S(2)}) async-start(bf16[16,128,200]{1,2,0:T(8,128)(2,1)} %fusion.18), calls=%async_computation | async-start | bytes 1638400 | tf_op jit(solution)/shard_map/all_to_all | solution.py:102
  305.8 0.8 dynamic_slice.15
  306.6 1.9 constant_dynamic-slice_fusion
  308.5 0.8 copy.37
  309.3 11.9 %all-to-all-done = bf16[16,128,200]{1,2,0:T(8,128)(2,1)S(1)} async-done(((bf16[16,128,200]{1,2,0:T(8,128)(2,1)}), bf16[16,128,200]{1,2,0:T(8,128)(2,1)S(1)}, u32[]{:S(2)}, u32[]{:S(2)}) %all-to-all-start) | async-done | bytes 819232 | tf_op jit(solution)/shard_map/all_to_all | solution.py:102
  321.3 25.5 %all-gather.10.cloned.1.call-done = bf16[34816,128]{1,0:T(8,128)(2,1)} async-done(((bf16[2176,128]{1,0:T(8,128)(2,1)}), bf16[34816,128]{1,0:T(8,128)(2,1)}) %all-gather.10.cloned.1.call-update) | async-done | bytes 8912912 | tf_op jit(solution)/shard_map/all_gather | solution.py:104
  346.8 10.8 %convolution_convert_fusion.1 = bf16[16,2176,200]{1,2,0:T(8,128)(2,1)} fusion(bf16[16,2176,128]{2,1,0:T(8,128)(2,1)} %bitcast.114, bf16[16,128,200]{1,2,0:T(8,128)(2,1)S(1)} %all-to-all-done), kind=kOutput, calls=%fused_computation.8 | convolution fusion | flops 1789542400 | bytes 23658496 | tf_op jit(solution)/shard_map/hsc,hcd->hsd/dot_general | solution.py:105
  357.6 7.3 %convert_reduce_fusion = f32[2176,200]{0,1:T(8,128)S(1)} fusion(bf16[16,2176,200]{1,2,0:T(8,128)(2,1)} %convolution_convert_fusion.1), kind=kLoop, calls=%fused_computation.7 | loop fusion | flops 13491200 | bytes 15667200 | tf_op jit(solution)/shard_map/reduce_sum | solution.py:111
  365.0 0.3 fusion.13
  365.3 0.4 fusion.46
  365.6 0.2 copy.30
  365.8 1.0 reshape.240
  366.9 0.2 copy.32
  367.1 1.1 reshape.241
  368.1 4.9 copy.33
  373.0 3.9 stack_reshape.7
  376.9 4.9 copy.31
  381.7 3.8 stack_reshape.6
  385.6 1.2 pad_maximum_fusion
  386.8 3.3 broadcast_select_fusion
  390.1 5.0 all-to-all-start.1
  395.1 0.1 reshape.245
  395.3 0.1 reduce
  395.4 90.6 %all-to-all-done.1 = bf16[8,2,256,800]{2,3,1,0:T(8,128)(2,1)} async-done(((bf16[8,2,256,800]{2,3,1,0:T(8,128)(2,1)}), bf16[8,2,256,800]{2,3,1,0:T(8,128)(2,1)}, u32[]{:S(2)}, u32[]{:S(2)}) %all-to-all-start.1) | async-done | bytes 6553632 | tf_op jit(solution)/shard_map/all_to_all | solution.py:122
  486.1 11.1 %copy.34 = bf16[8,2,256,800]{3,2,1,0:T(8,128)(2,1)} copy(bf16[8,2,256,800]{2,3,1,0:T(8,128)(2,1)} %all-to-all-done.1) | data formatting | bytes 13107200 | tf_op jit(solution)/shard_map/all_to_all | solution.py:122
  497.1 14.7 %reshape.242 = bf16[16,204800]{1,0:T(8,128)(2,1)} reshape(bf16[8,2,256,800]{3,2,1,0:T(8,128)(2,1)} %copy.34) | data formatting | bytes 13107200 | tf_op jit(solution)/shard_map/reshape | solution.py:39
  511.9 4.0 convolution_convert_fusion
  515.9 1.6 reshape.253
  517.5 2.8 reshape.243
  520.3 2.3 copy.35
  (28 shorter events, 0.5 us)
Async XLA Ops:
  6.5 103.6 %all-gather.8.cloned.1.call-start = ((), (), s32[]{:S(2)}) async-start(), calls=%async_computation.3 | async-start | bytes 14796800 | tf_op jit(solution)/shard_map/all_gather | solution.py:46
  7.3 158.4 %all-gather.6.cloned.1.call-start = ((), (), s32[]{:S(2)}) async-start(), calls=%async_computation.2 | async-start | bytes 2764800 | tf_op jit(solution)/shard_map/all_gather | solution.py:56
  8.0 338.8 %all-gather.10.cloned.1.call-start = ((), (), s32[]{:S(2)}) async-start(), calls=%async_computation.4 | async-start | bytes 9469952 | tf_op jit(solution)/shard_map/all_gather | solution.py:104
  8.8 156.8 %copy-start.4 = (f32[3200]{0:T(1024)S(1)}, f32[3200]{0:T(1024)}, u32[]{:S(2)}) copy-start(f32[3200]{0:T(1024)} %param.9) | copy-start | bytes 38404
  245.3 3.4 copy-start
  248.7 5.9 %copy-start.1 = (bf16[128,400]{0,1:T(8,128)(2,1)S(1)}, bf16[128,400]{0,1:T(8,128)(2,1)}, u32[]{:S(2)}) copy-start(bf16[128,400]{0,1:T(8,128)(2,1)} %param.12) | copy-start | bytes 307204
  253.6 52.0 %copy-start.2 = (s32[8,2]{0,1:T(2,128)S(1)}, s32[8,2]{0,1:T(2,128)}, u32[]{:S(2)}) copy-start(s32[8,2]{0,1:T(2,128)} %param.15) | copy-start | bytes 196
  253.6 52.0 %copy-start.3 = (s32[8,2]{0,1:T(2,128)S(1)}, s32[8,2]{0,1:T(2,128)}, u32[]{:S(2)}) copy-start(s32[8,2]{0,1:T(2,128)} %param.14) | copy-start | bytes 196
  290.0 31.3 %all-to-all-start = ((bf16[16,128,200]{1,2,0:T(8,128)(2,1)}), bf16[16,128,200]{1,2,0:T(8,128)(2,1)S(1)}, u32[]{:S(2)}, u32[]{:S(2)}) async-start(bf16[16,128,200]{1,2,0:T(8,128)(2,1)} %fusion.18), calls=%async_computation | async-start | bytes 1638400 | tf_op jit(solution)/shard_map/all_to_all | solution.py:102
  390.1 95.9 %all-to-all-start.1 = ((bf16[8,2,256,800]{2,3,1,0:T(8,128)(2,1)}), bf16[8,2,256,800]{2,3,1,0:T(8,128)(2,1)}, u32[]{:S(2)}, u32[]{:S(2)}) async-start(bf16[8,2,256,800]{2,3,1,0:T(8,128)(2,1)} %broadcast_select_fusion), calls=%async_computation.1 | async-start | bytes 13107200 | tf_op jit(solution)/shard_map/all_to_all | solution.py:122
Sparse Core Ops, SparseCore 0:
  9.8 100.3 all-gather.7
  111.8 53.8 all-gather.5
  254.7 92.0 all-gather.9
